TPU v7x, 128 devices: a whole 4x4x4 slice. The times are simulated.
128 devices in a mesh: seq: 32 (over x, z, y_lo), dp: 4 (over y_hi, core).
Axes of the slice: x: 4, y: 4 (y_hi: 2, y_lo: 2; y = y_hi * 2 + y_lo), z: 4, core: 2. Of those that a mesh axis runs over, the one named last changes fastest.
Arguments:
- signal: bfloat16 [65536, 128], P(('seq', 'dp')), may hold values from -6 to 6
- filter_param: bfloat16 [65536, 128], P(('seq', 'dp')), may hold values from -6 to 6
- skip_gain: float32 [128], replicated, may hold values from 0.5 to 1.5
- out_grad: bfloat16 [65536, 128], P(('seq', 'dp')), may hold values from -6 to 6
Outputs:
- conv_out: bfloat16 [65536, 128], P(('seq', 'dp'))
- input_grad: bfloat16 [65536, 128], P(('seq', 'dp'))
- filter_grad: float32 [65536, 128], P(('seq', 'dp'))
All inputs are finite; a program needn't handle non-finite values.
Results may differ from a plain program's by a relative error of at most 0.001.
Values may be sent and summed in bfloat16 or wider, within the bound.
No kernel may reach another device: no remote copies, remote signals or barrier semaphores. Data moves between devices by JAX's collectives and lax.ppermute only.
A program may use at most 64 MiB of HBM per device.

v0:
```python
import math
import numpy as np
import jax
import jax.numpy as jnp
from jax import lax
from jax.sharding import PartitionSpec as P

FIRST_LEN = 512
AXES = ("seq", "dp")
highest = lax.Precision.HIGHEST


def half_table(order):
    half = order // 2
    slot = np.arange(half)[:, None]
    pos = np.arange(order)[None, :]
    angle = slot * pos % order * (2.0 * np.pi / order)
    real_rows = np.cos(angle)
    imag_rows = -np.sin(angle)
    real_rows[0, :] = 1.0
    imag_rows[0, :] = np.where(np.arange(order) % 2 == 0, 1.0, -1.0)
    return jnp.asarray(np.concatenate([real_rows, imag_rows], axis=0), dtype=jnp.float32)


def full_table(order):
    idx = np.arange(order)
    angle = idx[:, None] * idx[None, :] % order * (2.0 * np.pi / order)
    c, s = (np.cos(angle), np.sin(angle))
    top = np.concatenate([c, s], axis=1)
    bottom = np.concatenate([-s, c], axis=1)
    return jnp.asarray(np.concatenate([top, bottom], axis=0), dtype=jnp.float32)


def rotate(re, im, cos_t, sin_t):
    return (re * cos_t - im * sin_t, re * sin_t + im * cos_t)


def per_device(signal, filter_param, skip_gain, out_grad):
    dev_count = lax.axis_size(AXES)
    me = lax.axis_index(AXES)
    tok_rows, chans = signal.shape
    length = tok_rows * dev_count
    first_len = FIRST_LEN
    second_len = length // first_len
    first_dev = first_len // dev_count
    half = first_len // 2
    slots = half // dev_count
    assert second_len == dev_count and slots * dev_count == half
    stacked = jnp.concatenate([signal, out_grad, filter_param], axis=1)
    blocks = stacked.reshape(first_dev, second_len, 3 * chans)
    columns = lax.all_to_all(blocks, AXES, split_axis=1, concat_axis=0, tiled=True)
    columns = columns.reshape(first_len, 3 * chans).astype(jnp.float32)
    table_a = half_table(first_len)
    part = jnp.dot(table_a, columns, precision=highest)
    part = part.reshape(2, dev_count, slots, 3 * chans)
    got = lax.all_to_all(part, AXES, split_axis=1, concat_axis=1, tiled=True)
    z_re, z_im = (got[0], got[1])
    pos_b = jnp.arange(second_len, dtype=jnp.float32)[:, None]
    freq = (me * slots + jnp.arange(slots, dtype=jnp.int32)).astype(jnp.float32)[None, :]
    phase = pos_b * freq * (-2.0 * math.pi / length)
    tw_c = jnp.cos(phase)[:, :, None]
    tw_s = jnp.sin(phase)[:, :, None]
    t_re, t_im = rotate(z_re, z_im, tw_c, tw_s)
    is_first = me == 0
    t_im0 = jnp.where(is_first, 0.0, t_im[:, 0:1])
    nyq_phase = pos_b * (-2.0 * math.pi * half / length)
    nyq_c = jnp.cos(nyq_phase)[:, :, None]
    nyq_s = jnp.sin(nyq_phase)[:, :, None]
    extra_re = jnp.where(is_first, z_im[:, 0:1] * nyq_c, 0.0)
    extra_im = jnp.where(is_first, z_im[:, 0:1] * nyq_s, 0.0)
    rows_re = jnp.concatenate([t_re, extra_re], axis=1)
    rows_im = jnp.concatenate([t_im0, t_im[:, 1:], extra_im], axis=1)
    nrows = slots + 1
    table_b = full_table(second_len)
    both = jnp.stack([rows_re, rows_im]).reshape(2 * second_len, nrows * 3 * chans)
    spec = jnp.dot(table_b, both, precision=highest).reshape(2, second_len, nrows, 3 * chans)
    sr, si = (spec[0], spec[1])
    sig_r, cot_r, flt_r = (sr[..., :chans], sr[..., chans : 2 * chans], sr[..., 2 * chans :])
    sig_i, cot_i, flt_i = (si[..., :chans], si[..., chans : 2 * chans], si[..., 2 * chans :])
    scale = 1.0 / (math.sqrt(length) * length)
    conv_r = (sig_r * flt_r - sig_i * flt_i) * scale
    conv_i = (sig_r * flt_i + sig_i * flt_r) * scale
    back_r = (flt_r * cot_r + flt_i * cot_i) * scale
    back_i = (flt_r * cot_i - flt_i * cot_r) * scale
    taps_r = (sig_r * cot_r + sig_i * cot_i) * scale
    taps_i = (sig_r * cot_i - sig_i * cot_r) * scale
    prod = jnp.stack(
        [
            jnp.concatenate([conv_r, back_r, taps_r], axis=-1),
            jnp.concatenate([conv_i, back_i, taps_i], axis=-1),
        ]
    ).reshape(2 * second_len, nrows * 3 * chans)
    unit = lax.dot_general(table_b, prod, (((0,), (0,)), ((), ())), precision=highest).reshape(
        2, second_len, nrows, 3 * chans
    )
    u_re, u_im = (unit[0], unit[1])
    v_re, v_im = rotate(u_re[:, :slots], u_im[:, :slots], tw_c, -tw_s)
    x_re, _ = rotate(u_re[:, slots:], u_im[:, slots:], nyq_c, -nyq_s)
    out_re0 = jnp.where(is_first, v_re[:, 0:1], 2.0 * v_re[:, 0:1])
    out_im0 = jnp.where(is_first, x_re, 2.0 * v_im[:, 0:1])
    out_re = jnp.concatenate([out_re0, 2.0 * v_re[:, 1:]], axis=1)
    out_im = jnp.concatenate([out_im0, 2.0 * v_im[:, 1:]], axis=1)
    back_part = jnp.stack([out_re, out_im])
    ret = lax.all_to_all(back_part, AXES, split_axis=1, concat_axis=1, tiled=True)
    ret = ret.reshape(first_len, 3 * chans)
    times = lax.dot_general(table_a, ret, (((0,), (0,)), ((), ())), precision=highest)
    conv_cols = times[:, :chans] + skip_gain * columns[:, :chans]
    back_cols = times[:, chans : 2 * chans] + skip_gain * columns[:, chans : 2 * chans]
    taps_cols = times[:, 2 * chans :]
    taps_hi = lax.reduce_precision(taps_cols, exponent_bits=8, mantissa_bits=7)
    taps_lo = taps_cols - taps_hi
    outs = jnp.concatenate(
        [
            conv_cols.astype(jnp.bfloat16),
            back_cols.astype(jnp.bfloat16),
            taps_hi.astype(jnp.bfloat16),
            taps_lo.astype(jnp.bfloat16),
        ],
        axis=1,
    ).reshape(dev_count, first_dev, 1, 4 * chans)
    rows = lax.all_to_all(outs, AXES, split_axis=0, concat_axis=2, tiled=True)
    rows = rows.reshape(tok_rows, 4 * chans)
    conv_out = rows[:, :chans]
    input_grad = rows[:, chans : 2 * chans]
    filter_grad = rows[:, 2 * chans : 3 * chans].astype(jnp.float32) + rows[:, 3 * chans :].astype(
        jnp.float32
    )
    return (conv_out, input_grad, filter_grad)


def solution(mesh):
    placed = (P(AXES, None), P(AXES, None), P(), P(AXES, None))
    return jax.shard_map(
        per_device,
        mesh=mesh,
        in_specs=placed,
        out_specs=(P(AXES, None), P(AXES, None), P(AXES, None)),
        check_vma=False,
    )
```

profile of v0, /device:TPU:1, one launch (start us, length us, event | category | flops | bytes accessed | tf_op | source)
XLA Modules:
  0.0 102.3 jit_solution(3189238744467558587)
XLA Ops:
  0.6 1.1 %pad_maximum_fusion.4 = bf16[512,384]{1,0:T(8,128)(2,1)S(1)} fusion(bf16[512,128]{1,0:T(8,128)(2,1)} %param.7, bf16[512,128]{1,0:T(8,128)(2,1)} %param.9, bf16[512,128]{1,0:T(8,128)(2,1)} %param.6), kind=kLoop, calls=%fused_computation.15 | loop fusion | flops 1179648 | bytes 786432 | tf_op jit(solution)/shard_map/concatenate | solution.py:49
  1.7 0.3 copy.52
  2.0 23.5 %all_to_all.40 = bf16[4,128,384]{2,0,1:T(4,128)(2,1)S(1)} all-to-all(bf16[4,128,384]{2,0,1:T(4,128)(2,1)S(1)} %copy.52), channel_id=1, replica_groups=mesh['seq'=32,'dp'=4] {'seq','dp'}, dimensions={1} | all-to-all | bytes 786432 | tf_op jit(solution)/shard_map/all_to_all | solution.py:51
  25.6 1.0 fusion.24
  26.6 0.5 reshape.132
  27.1 1.1 %copy.54 = f32[2,128,2,384]{3,2,0,1:T(2,128)} copy(f32[2,128,2,384]{3,2,1,0:T(2,128)S(1)} %reshape.132) | data formatting | bytes 1572864 | tf_op jit(solution)/shard_map/reshape | solution.py:55
  28.3 4.4 %all-to-all-start.1 = ((f32[2,128,2,384]{3,2,0,1:T(2,128)}), f32[2,128,2,384]{3,2,0,1:T(2,128)S(1)}, u32[]{:S(2)}, u32[]{:S(2)}) async-start(f32[2,128,2,384]{3,2,0,1:T(2,128)} %copy.54), calls=%async_computation.1 | async-start | bytes 1572864 | tf_op jit(solution)/shard_map/all_to_all | solution.py:56
  32.9 16.1 %all-to-all-done.1 = f32[2,128,2,384]{3,2,0,1:T(2,128)S(1)} async-done(((f32[2,128,2,384]{3,2,0,1:T(2,128)}), f32[2,128,2,384]{3,2,0,1:T(2,128)S(1)}, u32[]{:S(2)}, u32[]{:S(2)}) %all-to-all-start.1) | async-done | bytes 786464 | tf_op jit(solution)/shard_map/all_to_all | solution.py:56
  49.0 0.3 fusion.22
  50.0 0.9 copy.57
  51.0 1.3 %fusion.3 = f32[256,1152]{1,0:T(8,128)S(1)} fusion(f32[256,256]{1,0:T(8,128)S(1)} %copy-done, f32[144,8,2,128]{3,2,1,0:T(2,128)S(1)} %bitcast.66), kind=kOutput, calls=%fused_computation.3 | convolution fusion | flops 905969664 | bytes 2621440 | tf_op jit(solution)/shard_map/dot_general | solution.py:76
  53.2 0.9 copy.60
  54.1 2.2 %fusion = f32[256,1152]{1,0:T(8,128)S(1)} fusion(f32[256,256]{1,0:T(8,128)S(1)} %copy-done, f32[144,8,2,128]{3,2,1,0:T(2,128)S(1)} %bitcast.65), kind=kOutput, calls=%fused_computation | convolution fusion | flops 905969664 | bytes 2621440 | tf_op jit(solution)/shard_map/dot_general | solution.py:93
  57.2 1.2 %copy.63 = f32[2,128,2,384]{3,2,0,1:T(2,128)} copy(f32[2,128,2,384]{1,3,2,0:T(8,128)S(1)} %pad_maximum_fusion.2) | data formatting | bytes 1572864 | tf_op jit(solution)/shard_map/stack | solution.py:103
  58.4 4.8 %all-to-all-start.2 = ((f32[2,128,2,384]{3,2,0,1:T(2,128)}), f32[2,128,2,384]{3,2,0,1:T(2,128)S(1)}, u32[]{:S(2)}, u32[]{:S(2)}) async-start(f32[2,128,2,384]{3,2,0,1:T(2,128)} %copy.63), calls=%async_computation.2 | async-start | bytes 1572864 | tf_op jit(solution)/shard_map/all_to_all | solution.py:104
  63.4 0.3 reshape.142
  64.0 15.6 %all-to-all-done.2 = f32[2,128,2,384]{3,2,0,1:T(2,128)S(1)} async-done(((f32[2,128,2,384]{3,2,0,1:T(2,128)}), f32[2,128,2,384]{3,2,0,1:T(2,128)S(1)}, u32[]{:S(2)}, u32[]{:S(2)}) %all-to-all-start.2) | async-done | bytes 786464 | tf_op jit(solution)/shard_map/all_to_all | solution.py:104
  79.6 0.3 copy.64
  79.9 0.5 reshape.135
  80.4 0.7 copy-done.1
  81.1 1.5 %fusion.25 = f32[512,384]{0,1:T(8,128)S(1)} fusion(f32[512,512]{1,0:T(8,128)S(1)} %copy-done.1, f32[512,384]{1,0:T(8,128)S(1)} %reshape.135), kind=kOutput, calls=%fused_computation.64 | convolution fusion | flops 1207959552 | bytes 2621440 | tf_op jit(solution)/shard_map/dot_general | solution.py:106
  83.1 17.6 %all_to_all.41 = bf16[128,4,1,512]{3,1,2,0:T(4,128)(2,1)S(1)} all-to-all(bf16[128,4,1,512]{3,1,2,0:T(4,128)(2,1)S(1)} %bitcast.74), channel_id=1, replica_groups=mesh['seq'=32,'dp'=4] {'seq','dp'}, dimensions={0} | all-to-all | bytes 1048576 | tf_op jit(solution)/shard_map/all_to_all | solution.py:121
  100.8 0.7 fusion.23
  101.6 0.7 convert_add_fusion
  (46 shorter events, 3.8 us)
Async XLA Ops:
  1.7 23.9 %copy-start.2 = (f32[512,512]{1,0:T(8,128)S(1)}, f32[512,512]{1,0:T(8,128)}, u32[]{:S(2)}) copy-start(f32[512,512]{1,0:T(8,128)} %constant.33) | copy-start | bytes 3145732
  28.3 20.7 %all-to-all-start.1 = ((f32[2,128,2,384]{3,2,0,1:T(2,128)}), f32[2,128,2,384]{3,2,0,1:T(2,128)S(1)}, u32[]{:S(2)}, u32[]{:S(2)}) async-start(f32[2,128,2,384]{3,2,0,1:T(2,128)} %copy.54), calls=%async_computation.1 | async-start | bytes 1572864 | tf_op jit(solution)/shard_map/all_to_all | solution.py:56
  50.0 1.0 copy-start
  58.4 21.2 %all-to-all-start.2 = ((f32[2,128,2,384]{3,2,0,1:T(2,128)}), f32[2,128,2,384]{3,2,0,1:T(2,128)S(1)}, u32[]{:S(2)}, u32[]{:S(2)}) async-start(f32[2,128,2,384]{3,2,0,1:T(2,128)} %copy.63), calls=%async_computation.2 | async-start | bytes 1572864 | tf_op jit(solution)/shard_map/all_to_all | solution.py:104
  79.9 1.2 %copy-start.1 = (f32[512,512]{1,0:T(8,128)S(1)}, f32[512,512]{1,0:T(8,128)}, u32[]{:S(2)}) copy-start(f32[512,512]{1,0:T(8,128)} %constant.29.clone) | copy-start | bytes 3145732
  81.1 1.5 %copy-start.3 = (f32[128]{0:T(128)S(1)}, f32[128]{0:T(128)}, u32[]{:S(2)}) copy-start(f32[128]{0:T(128)} %param.8) | copy-start | bytes 1540
where the time goes:
time: 103 us; the launch traced here: 102 us
  blocking collectives  41.2 us (40%)
  waiting for transfers between devices  31.7 us (31%)
  local copies, waits for them, and re-layouts  9.97 us (10%)
  starting transfers between devices  9.18 us (9%)
  matrix products  5.95 us (6%)
  other arithmetic  3.32 us (3%)
    all_to_all x1, blocking collectives, per_device(): lax.all_to_all(blocks, AXES, split_axis=1, concat_axis=0, tiled=True)  23.5 us
    all_to_all x1, blocking collectives, per_device(): rows = lax.all_to_all(outs, AXES, split_axis=0, concat_axis=2, tiled=True)  17.6 us
    all_to_all x1, waiting for transfers between devices, per_device(): got = lax.all_to_all(part, AXES, split_axis=1, concat_axis=1, tiled=True)  16.1 us
    all_to_all x1, waiting for transfers between devices, per_device(): lax.all_to_all(back_part, AXES, split_axis=1, concat_axis=1, tiled=True)  15.6 us
    all_to_all x1, starting transfers between devices, per_device(): lax.all_to_all(back_part, AXES, split_axis=1, concat_axis=1, tiled=True)  4.83 us
    all_to_all x1, starting transfers between devices, per_device(): got = lax.all_to_all(part, AXES, split_axis=1, concat_axis=1, tiled=True)  4.36 us
    dot_general x1, matrix products, per_device(): lax.dot_general(table_b, prod, (((0,), (0,)), ((), ())), precision=highest)  2.23 us
  transfers between devices with their start and end apart: 2, of which 2 were waited for; matrix products, arithmetic and copies ran while one was open for 1% of the time, Pallas kernels for 0%

commit v1 on v0

--- a/solution.py
+++ b/solution.py
@@ -8,6 +8,12 @@
 FIRST_LEN = 512
 AXES = ("seq", "dp")
 highest = lax.Precision.HIGHEST
+
+
+def trade_parts(block, name, split, join):
+    pieces = jnp.split(block, lax.axis_size(name), axis=split)
+    received = lax.all_to_all(jnp.stack(pieces), name, 0, 0)
+    return jnp.concatenate(received, axis=join)
 
 
 def half_table(order):
@@ -53,7 +59,7 @@
     table_a = half_table(first_len)
     part = jnp.dot(table_a, columns, precision=highest)
     part = part.reshape(2, dev_count, slots, 3 * chans)
-    got = lax.all_to_all(part, AXES, split_axis=1, concat_axis=1, tiled=True)
+    got = trade_parts(part, AXES, 1, 1)
     z_re, z_im = (got[0], got[1])
     pos_b = jnp.arange(second_len, dtype=jnp.float32)[:, None]
     freq = (me * slots + jnp.arange(slots, dtype=jnp.int32)).astype(jnp.float32)[None, :]

time: 103 us -> 182 us (1.77)
  local copies, waits for them, and re-layouts: 9.97 us -> 85.3 us
  other arithmetic: 3.32 us -> 7.65 us
    unnamed x12 -> x142, local copies, waits for them, and re-layouts: 1.35 us -> 77.9 us
where the time goes in v1:
time: 182 us
  local copies, waits for them, and re-layouts  85.3 us (47%)
  blocking collectives  41.2 us (23%)
  waiting for transfers between devices  31.4 us (17%)
  starting transfers between devices  9.23 us (5%)
  other arithmetic  7.65 us (4%)
  matrix products  5.93 us (3%)
    unnamed x142, local copies, waits for them, and re-layouts  77.9 us
    all_to_all x1, blocking collectives, per_device(): lax.all_to_all(blocks, AXES, split_axis=1, concat_axis=0, tiled=True)  23.5 us
    all_to_all x1, blocking collectives, per_device(): rows = lax.all_to_all(outs, AXES, split_axis=0, concat_axis=2, tiled=True)  17.6 us
    all_to_all x1, waiting for transfers between devices, trade_parts(): received = lax.all_to_all(jnp.stack(pieces), name, 0, 0)  15.7 us
    all_to_all x1, waiting for transfers between devices, per_device(): lax.all_to_all(back_part, AXES, split_axis=1, concat_axis=1, tiled=True)  15.6 us
    all_to_all x1, starting transfers between devices, per_device(): lax.all_to_all(back_part, AXES, split_axis=1, concat_axis=1, tiled=True)  4.87 us
    all_to_all x1, starting transfers between devices, trade_parts(): received = lax.all_to_all(jnp.stack(pieces), name, 0, 0)  4.37 us
  transfers between devices with their start and end apart: 2, of which 2 were waited for; matrix products, arithmetic and copies ran while one was open for 1% of the time, Pallas kernels for 0%

profile of v1, /device:TPU:1, one launch (start us, length us, event | category | flops | bytes accessed | tf_op | source)
XLA Modules:
  0.0 181.7 jit_solution(5678261300418839187)
XLA Ops:
  0.6 1.1 pad_maximum_fusion.4
  2.0 23.5 %all_to_all.40 = bf16[4,128,384]{2,0,1:T(4,128)(2,1)S(1)} all-to-all(bf16[4,128,384]{2,0,1:T(4,128)(2,1)S(1)} %copy.716), channel_id=1, replica_groups=mesh['seq'=32,'dp'=4] {'seq','dp'}, dimensions={1} | all-to-all | bytes 786432 | tf_op jit(solution)/shard_map/all_to_all | solution.py:57
  25.6 1.0 fusion.16
  27.1 0.6 constant_dynamic-update-slice_fusion.127
  29.5 0.6 constant_dynamic-update-slice_fusion.123
  48.5 0.6 constant_dynamic-update-slice_fusion.91
  62.1 0.6 constant_dynamic-update-slice_fusion.68
  70.4 0.6 constant_dynamic-update-slice_fusion.54
  100.7 0.6 constant_dynamic-update-slice_fusion.3
  103.1 4.4 %all-to-all-start.1 = ((f32[128,2,1,2,384]{4,3,1,2,0:T(2,128)}), f32[128,2,1,2,384]{4,3,1,2,0:T(2,128)S(1)}, u32[]{:S(2)}, u32[]{:S(2)}) async-start(f32[128,2,1,2,384]{4,3,1,2,0:T(2,128)} %constant_dynamic-update-slice_fusion), calls=%async_computation.1 | async-start | bytes 1572864 | tf_op jit(solution)/shard_map/all_to_all | solution.py:15
  108.1 15.7 %all-to-all-done.1 = f32[128,2,1,2,384]{4,3,1,2,0:T(2,128)S(1)} async-done(((f32[128,2,1,2,384]{4,3,1,2,0:T(2,128)}), f32[128,2,1,2,384]{4,3,1,2,0:T(2,128)S(1)}, u32[]{:S(2)}, u32[]{:S(2)}) %all-to-all-start.1) | async-done | bytes 786464 | tf_op jit(solution)/shard_map/all_to_all | solution.py:15
  126.4 0.8 copy-done
  127.2 1.2 fusion.17
  129.4 0.9 copy.852
  130.3 2.2 %fusion = f32[256,1152]{1,0:T(8,128)S(1)} fusion(f32[256,256]{1,0:T(8,128)S(1)} %copy-done, f32[144,8,2,128]{3,2,1,0:T(2,128)S(1)} %bitcast.838), kind=kOutput, calls=%fused_computation.1 | convolution fusion | flops 905969664 | bytes 2621440 | tf_op jit(solution)/shard_map/dot_general | solution.py:99
  134.4 1.2 broadcast_select_fusion
  136.7 1.2 copy.860
  137.8 4.9 %all-to-all-start.2 = ((f32[2,128,2,384]{3,2,0,1:T(2,128)}), f32[2,128,2,384]{3,2,0,1:T(2,128)S(1)}, u32[]{:S(2)}, u32[]{:S(2)}) async-start(f32[2,128,2,384]{3,2,0,1:T(2,128)} %copy.860), calls=%async_computation.2 | async-start | bytes 1572864 | tf_op jit(solution)/shard_map/all_to_all | solution.py:110
  143.4 15.6 %all-to-all-done.2 = f32[2,128,2,384]{3,2,0,1:T(2,128)S(1)} async-done(((f32[2,128,2,384]{3,2,0,1:T(2,128)}), f32[2,128,2,384]{3,2,0,1:T(2,128)S(1)}, u32[]{:S(2)}, u32[]{:S(2)}) %all-to-all-start.2) | async-done | bytes 786464 | tf_op jit(solution)/shard_map/all_to_all | solution.py:110
  159.9 0.7 copy-done.1
  160.6 1.5 fusion.18
  162.6 17.6 %all_to_all.41 = bf16[128,4,1,512]{3,1,2,0:T(4,128)(2,1)S(1)} all-to-all(bf16[128,4,1,512]{3,1,2,0:T(4,128)(2,1)S(1)} %bitcast.846), channel_id=1, replica_groups=mesh['seq'=32,'dp'=4] {'seq','dp'}, dimensions={0} | all-to-all | bytes 1048576 | tf_op jit(solution)/shard_map/all_to_all | solution.py:127
  180.3 0.7 fusion.15
  181.0 0.7 convert_add_fusion
  (182 shorter events, 82.0 us)
Async XLA Ops:
  1.7 23.9 %copy-start.2 = (f32[512,512]{1,0:T(8,128)S(1)}, f32[512,512]{1,0:T(8,128)}, u32[]{:S(2)}) copy-start(f32[512,512]{1,0:T(8,128)} %constant.33) | copy-start | bytes 3145732
  103.1 20.7 %all-to-all-start.1 = ((f32[128,2,1,2,384]{4,3,1,2,0:T(2,128)}), f32[128,2,1,2,384]{4,3,1,2,0:T(2,128)S(1)}, u32[]{:S(2)}, u32[]{:S(2)}) async-start(f32[128,2,1,2,384]{4,3,1,2,0:T(2,128)} %constant_dynamic-update-slice_fusion), calls=%async_computation.1 | async-start | bytes 1572864 | tf_op jit(solution)/shard_map/all_to_all | solution.py:15
  126.3 1.0 copy-start
  137.8 21.2 %all-to-all-start.2 = ((f32[2,128,2,384]{3,2,0,1:T(2,128)}), f32[2,128,2,384]{3,2,0,1:T(2,128)S(1)}, u32[]{:S(2)}, u32[]{:S(2)}) async-start(f32[2,128,2,384]{3,2,0,1:T(2,128)} %copy.860), calls=%async_computation.2 | async-start | bytes 1572864 | tf_op jit(solution)/shard_map/all_to_all | solution.py:110
  159.3 1.2 copy-start.1
  160.6 1.5 copy-start.3
